TPU v7x, 32 devices: a whole 2x2x4 slice. The times are simulated.
32 devices in a mesh: gz: 4 (over x, core), gy: 4 (over z), gx: 2 (over y).
Axes of the slice: x: 2, y: 2, z: 4, core: 2. Of those that a mesh axis runs over, the one named last changes fastest.
Arguments:
- volume: bfloat16 [32, 4, 32, 384], P('gz', 'gy', 'gx'), may hold values from -80 to 80
- cotangent: bfloat16 [32, 4, 32, 384], P('gz', 'gy', 'gx'), may hold values from -6 to 6
- w_project: bfloat16 [3, 384, 1152], P(None, 'gy', ('gz', 'gx')), may hold values from -0.3125 to 0.3125
- w_output: bfloat16 [3, 384, 384], P(None, 'gy', ('gz', 'gx')), may hold values from -0.3125 to 0.3125
Outputs:
- grad_volume: bfloat16 [32, 4, 32, 384], P('gz', 'gy', 'gx')
All inputs are finite; a program needn't handle non-finite values.
Results may differ from a plain program's by a relative error of at most 0.015.
Values may be sent and summed in bfloat16 or wider, within the bound.
No kernel may reach another device: no remote copies, remote signals or barrier semaphores. Data moves between devices by JAX's collectives and lax.ppermute only.
A program may use at most 64 MiB of HBM per device.

v0:
```python
import jax
import jax.numpy as jnp
from jax import lax
from jax.sharding import PartitionSpec as P

HEADS = 6
ALL = ("gz", "gy", "gx")


def head_norm(vector):
    return (vector * lax.rsqrt(jnp.mean(vector * vector, axis=-1, keepdims=True) + 1e-06)).astype(
        jnp.bfloat16
    )


def sublayer(line_rows, w_inner, w_outer):
    feat_len = line_rows.shape[-1]
    head_size = feat_len // HEADS
    stream = line_rows.astype(jnp.float32)
    normed = (stream * lax.rsqrt(jnp.mean(stream * stream, axis=-1, keepdims=True) + 1e-06)).astype(
        jnp.bfloat16
    )
    packed = jnp.dot(normed, w_inner, preferred_element_type=jnp.float32)
    head_shape = line_rows.shape[:3] + (HEADS, head_size)
    queries = head_norm(packed[..., :feat_len].reshape(head_shape))
    key_part = head_norm(packed[..., feat_len : 2 * feat_len].reshape(head_shape))
    value_part = packed[..., 2 * feat_len :].reshape(head_shape).astype(jnp.bfloat16)
    scores = jnp.einsum(
        "plqhe,pkqhe->pqhlk", queries, key_part, preferred_element_type=jnp.float32
    ) * head_size ** (-0.5)
    powers = jnp.exp(scores)
    attn_weights = (powers / jnp.sum(powers, axis=-1, keepdims=True)).astype(jnp.bfloat16)
    mixed_out = jnp.einsum(
        "pqhlk,pkqhe->plqhe", attn_weights, value_part, preferred_element_type=jnp.float32
    )
    mixed_out = mixed_out.astype(jnp.bfloat16).reshape(line_rows.shape)
    update = jnp.dot(mixed_out, w_outer, preferred_element_type=jnp.float32)
    return (stream + update).astype(jnp.bfloat16)


def full_weights(w_project, w_output, index, sizes):
    nz, ny, nx = sizes
    proj, outp = (w_project[index], w_output[index])
    din, dproj = proj.shape
    cat = jnp.concatenate([proj, outp], axis=1)
    got = lax.all_gather(cat, ALL, axis=0, tiled=False)
    got = got.reshape(nz, ny, nx, din, cat.shape[1])
    got = jnp.transpose(got, (1, 3, 0, 2, 4)).reshape(ny * din, nz * nx, cat.shape[1])
    w_inner = got[:, :, :dproj].reshape(ny * din, nz * nx * dproj)
    w_outer = got[:, :, dproj:].reshape(ny * din, -1)
    return (w_inner, w_outer)


def depth_fn(member, w_inner, w_outer):
    depth_len, row_len, rest_len, feat_len = member.shape
    flat_lines = member.reshape(1, depth_len, row_len * rest_len, feat_len)
    return sublayer(flat_lines, w_inner, w_outer).reshape(member.shape)


def plane_fn(plane, w_row, w_col):
    after_rows = sublayer(plane[None], *w_row)[0]
    return sublayer(after_rows[:, :, None, :], *w_col)[:, :, 0, :]


def to_planes(depth_lines, sizes):
    nz, ny, nx = sizes
    z_len, yl, kx, feat = depth_lines.shape
    got = lax.all_to_all(depth_lines, ALL, 0, 0, tiled=True)
    got = got.reshape(nz, ny, nx, yl, kx, feat)
    return jnp.transpose(got, (1, 3, 2, 0, 4, 5)).reshape(ny * yl, nx * nz * kx, feat)


def from_planes(plane, sizes):
    nz, ny, nx = sizes
    rows, cols, feat = plane.shape
    yl, kx = (rows // ny, cols // (nx * nz))
    parts = plane.reshape(ny, yl, nx, nz, kx, feat)
    parts = jnp.transpose(parts, (3, 0, 2, 1, 4, 5)).reshape(nz * ny * nx, yl, kx, feat)
    return lax.all_to_all(parts, ALL, 0, 0, tiled=True)


def block_to_plane(block, sizes):
    nz, ny, nx = sizes
    zl, yl, xl, feat = block.shape
    got = lax.all_to_all(block, ("gy", "gx"), 0, 0, tiled=True)
    got = got.reshape(ny, nx, yl, xl, feat)
    return jnp.transpose(got, (0, 2, 1, 3, 4)).reshape(ny * yl, nx * xl, feat)


def local(volume, cotangent, w_project, w_output, sizes):
    w_depth = full_weights(w_project, w_output, 0, sizes)
    w_row = full_weights(w_project, w_output, 1, sizes)
    w_col = full_weights(w_project, w_output, 2, sizes)
    depth_act = lax.all_to_all(volume, "gz", 2, 0, tiled=True)
    cot_plane = block_to_plane(cotangent, sizes)
    field_one, depth_pullback = jax.vjp(lambda m: depth_fn(m, *w_depth), depth_act)
    plane_one = to_planes(field_one, sizes)
    _, plane_pullback = jax.vjp(lambda p: plane_fn(p, w_row, w_col), plane_one)
    grad_plane = plane_pullback(cot_plane)[0]
    grad_one = from_planes(grad_plane, sizes)
    grad_zero = depth_pullback(grad_one)[0]
    return lax.all_to_all(grad_zero, "gz", 0, 2, tiled=True)


def along_rows(member, w_inner, w_outer):
    return sublayer(member, w_inner, w_outer)


def along_columns(member, w_inner, w_outer):
    depth_len, row_len, col_len, feat_len = member.shape
    flat_lines = member.reshape(depth_len * row_len, col_len, 1, feat_len)
    return sublayer(flat_lines, w_inner, w_outer).reshape(member.shape)


def line_swap(stacked, axis, split_axis, concat_axis):
    return lax.all_to_all(stacked, axis, split_axis=split_axis, concat_axis=concat_axis, tiled=True)


def local_general(volume, cotangent, w_project, w_output, sizes):
    w_depth = full_weights(w_project, w_output, 0, sizes)
    w_row = full_weights(w_project, w_output, 1, sizes)
    w_col = full_weights(w_project, w_output, 2, sizes)

    def row_fn(member):
        return along_rows(member, *w_row)

    def column_fn(member):
        return along_columns(member, *w_col)

    depth_act = line_swap(volume, "gz", 2, 0)
    field_one, depth_pullback = jax.vjp(lambda m: depth_fn(m, *w_depth), depth_act)
    field_one = line_swap(field_one, "gz", 0, 2)
    row_act = line_swap(field_one, "gy", 2, 1)
    field_two, row_pullback = jax.vjp(row_fn, row_act)
    field_two = line_swap(field_two, "gy", 1, 2)
    paired = line_swap(jnp.stack([cotangent, field_two]), "gx", 1, 3)
    _, column_pullback = jax.vjp(column_fn, paired[1])
    grad_two = line_swap(column_pullback(paired[0])[0], "gx", 2, 0)
    grad_one = line_swap(row_pullback(line_swap(grad_two, "gy", 2, 1))[0], "gy", 1, 2)
    grad_zero = depth_pullback(line_swap(grad_one, "gz", 2, 0))[0]
    return line_swap(grad_zero, "gz", 0, 2)


def solution(mesh):
    sizes = (mesh.shape["gz"], mesh.shape["gy"], mesh.shape["gx"])

    def body(volume, *rest):
        one_depth = volume.shape[0] * sizes[0] == mesh.size
        return (local if one_depth else local_general)(volume, *rest, sizes)

    return jax.shard_map(
        body,
        mesh=mesh,
        in_specs=(
            P("gz", "gy", "gx", None),
            P("gz", "gy", "gx", None),
            P(None, "gy", ("gz", "gx")),
            P(None, "gy", ("gz", "gx")),
        ),
        out_specs=P("gz", "gy", "gx", None),
        check_vma=False,
    )
```

profile of v0, /device:TPU:0, one launch (start us, length us, event | category | flops | bytes accessed | tf_op | source)
XLA Modules:
  0.0 310.3 jit_solution(6159842277848257346)
XLA Ops:
  11.9 8.3 %all_to_all.42 = bf16[8,1,16,384]{3,0,1,2:T(8,128)(2,1)S(1)} all-to-all(bf16[8,1,16,384]{3,0,1,2:T(8,128)(2,1)S(1)} %copy.516), channel_id=1, replica_groups=mesh['gz'=4,'gy'=4,'gx'=2] {'gz'}, dimensions={2} | all-to-all | bytes 196608 | tf_op jit(solution)/shard_map/all_to_all | solution.py:94
  20.3 5.8 %all-to-all-start = ((bf16[8,1,16,384]{3,2,1,0:T(8,128)(2,1)}), bf16[8,1,16,384]{3,2,1,0:T(8,128)(2,1)S(1)}, u32[]{:S(2)}, u32[]{:S(2)}) async-start(bf16[8,1,16,384]{3,2,1,0:T(8,128)(2,1)} %param.5), calls=%async_computation | async-start | bytes 196608 | tf_op jit(solution)/shard_map/all_to_all | solution.py:85
  26.9 41.2 %all-gather.9.cloned.1.call-done = bf16[3072,192]{1,0:T(8,128)(2,1)} async-done(((bf16[96,192]{1,0:T(8,128)(2,1)}), bf16[3072,192]{1,0:T(8,128)(2,1)}) %all-gather.9.cloned.1.call-update) | async-done | bytes 1179664 | tf_op jit(solution)/shard_map/all_gather | solution.py:46
  68.1 2.8 copy.522
  75.3 1.8 convert_element_type.403
  85.7 39.3 %all-gather.11.cloned.1.call-done = bf16[3072,192]{1,0:T(8,128)(2,1)} async-done(((bf16[96,192]{1,0:T(8,128)(2,1)}), bf16[3072,192]{1,0:T(8,128)(2,1)}) %all-gather.11.cloned.1.call-update) | async-done | bytes 1179664 | tf_op jit(solution)/shard_map/all_gather | solution.py:46
  125.0 2.8 copy.538
  129.7 52.1 %all-gather.7.cloned.1.call-done = bf16[3072,192]{1,0:T(8,128)(2,1)} async-done(((bf16[96,192]{1,0:T(8,128)(2,1)}), bf16[3072,192]{1,0:T(8,128)(2,1)}) %all-gather.7.cloned.1.call-update) | async-done | bytes 1179664 | tf_op jit(solution)/shard_map/all_gather | solution.py:46
  181.9 2.8 copy.514
  184.7 1.9 reshape.948
  191.3 3.7 %all-to-all-start.2 = ((bf16[32,1,4,384]{3,2,1,0:T(4,128)(2,1)}), bf16[32,1,4,384]{3,2,1,0:T(4,128)(2,1)S(1)}, u32[]{:S(2)}, u32[]{:S(2)}) async-start(bf16[32,1,4,384]{3,2,1,0:T(4,128)(2,1)} %copy.534), calls=%async_computation.2 | async-start | bytes 196608 | tf_op jit(solution)/shard_map/all_to_all | solution.py:68
  196.2 6.3 %all-to-all-done.2 = bf16[32,1,4,384]{3,2,1,0:T(4,128)(2,1)S(1)} async-done(((bf16[32,1,4,384]{3,2,1,0:T(4,128)(2,1)}), bf16[32,1,4,384]{3,2,1,0:T(4,128)(2,1)S(1)}, u32[]{:S(2)}, u32[]{:S(2)}) %all-to-all-start.2) | async-done | bytes 98336 | tf_op jit(solution)/shard_map/all_to_all | solution.py:68
  214.3 1.8 convert_element_type.418
  221.7 1.8 reshape.969
  227.4 1.9 reshape.973
  229.3 1.9 multiply_reduce_fusion.1
  234.7 1.8 reshape.972
  236.6 1.9 reshape.975
  238.4 1.9 multiply_reduce_fusion
  243.9 1.8 reshape.974
  245.7 1.8 convert_element_type.434
  251.4 1.7 multiply_reduce_fusion.10
  253.1 1.6 multiply_reduce_fusion.11
  255.5 1.8 reshape.976
  261.9 1.9 reshape.977
  266.2 1.9 reshape.978
  268.1 1.6 multiply_reduce_fusion.14
  271.1 2.0 fusion.14
  273.1 1.6 multiply_reduce_fusion.9
  281.2 2.6 all-to-all-start.3
  283.8 7.6 %all-to-all-done.3 = bf16[32,1,4,384]{3,2,1,0:T(4,128)(2,1)S(1)} async-done(((bf16[32,1,4,384]{3,2,1,0:T(4,128)(2,1)}), bf16[32,1,4,384]{3,2,1,0:T(4,128)(2,1)S(1)}, u32[]{:S(2)}, u32[]{:S(2)}) %all-to-all-start.3) | async-done | bytes 98336 | tf_op jit(solution)/shard_map/all_to_all | solution.py:79
  296.4 6.7 %all_to_all.43 = bf16[32,1,4,384]{3,2,1,0:T(4,128)(2,1)S(1)} all-to-all(bf16[32,1,4,384]{3,2,1,0:T(4,128)(2,1)S(1)} %copy.626), channel_id=1, replica_groups=mesh['gz'=4,'gy'=4,'gx'=2] {'gz'}, dimensions={0} | all-to-all | bytes 196608 | tf_op jit(solution)/shard_map/all_to_all | solution.py:102
  (292 shorter events, 79.6 us)
Async XLA Ops:
  6.5 61.5 %all-gather.9.cloned.1.call-start = ((), (), s32[]{:S(2)}) async-start(), calls=%async_computation.6 | async-start | bytes 1622016 | tf_op jit(solution)/shard_map/all_gather | solution.py:46
  9.0 115.9 %all-gather.11.cloned.1.call-start = ((), (), s32[]{:S(2)}) async-start(), calls=%async_computation.7 | async-start | bytes 1622016 | tf_op jit(solution)/shard_map/all_gather | solution.py:46
  10.0 171.8 %all-gather.7.cloned.1.call-start = ((), (), s32[]{:S(2)}) async-start(), calls=%async_computation.5 | async-start | bytes 1622016 | tf_op jit(solution)/shard_map/all_gather | solution.py:46
  20.3 170.1 %copy-start.11 = (bf16[8,1,16,384]{3,0,1,2:T(8,128)(2,1)}, bf16[8,1,16,384]{3,0,1,2:T(8,128)(2,1)S(1)}, u32[]{:S(2)}) copy-start(bf16[8,1,16,384]{3,0,1,2:T(8,128)(2,1)S(1)} %all_to_all.42) | copy-start | bytes 294916
  20.3 171.1 %all-to-all-start = ((bf16[8,1,16,384]{3,2,1,0:T(8,128)(2,1)}), bf16[8,1,16,384]{3,2,1,0:T(8,128)(2,1)S(1)}, u32[]{:S(2)}, u32[]{:S(2)}) async-start(bf16[8,1,16,384]{3,2,1,0:T(8,128)(2,1)} %param.5), calls=%async_computation | async-start | bytes 196608 | tf_op jit(solution)/shard_map/all_to_all | solution.py:85
  74.0 9.7 %copy-start = (f32[1,32,4,6,64]{4,3,1,2,0:T(8,128)}, f32[1,32,4,6,64]{4,3,1,2,0:T(8,128)S(1)}, u32[]{:S(2)}) copy-start(f32[1,32,4,6,64]{4,3,1,2,0:T(8,128)S(1)} %reshape.958) | copy-start | bytes 589828
  83.9 41.0 %copy-start.16 = (f32[4,6,32,32]{2,3,1,0:T(8,128)}, f32[4,6,32,32]{2,3,1,0:T(8,128)S(1)}, u32[]{:S(2)}) copy-start(f32[4,6,32,32]{2,3,1,0:T(8,128)S(1)} %get-tuple-element.26) | copy-start | bytes 294916
  84.0 43.8 %copy-start.53 = (f32[4,6,32]{2,1,0:T(8,128)}, f32[4,6,32]{2,1,0:T(8,128)S(1)}, u32[]{:S(2)}) copy-start(f32[4,6,32]{2,1,0:T(8,128)S(1)} %get-tuple-element.25) | copy-start | bytes 9220
  186.6 2.9 copy-start.41
  186.6 3.5 %copy-start.38 = (bf16[1,32,4,6,64]{4,1,3,2,0:T(8,128)(2,1)S(1)}, bf16[1,32,4,6,64]{4,1,3,2,0:T(8,128)(2,1)}, u32[]{:S(2)}) copy-start(bf16[1,32,4,6,64]{4,1,3,2,0:T(8,128)(2,1)} %fusion.6) | copy-start | bytes 294916
  186.6 3.8 %copy-start.9 = (bf16[384,8,48]{0,2,1:T(8,128)(2,1)S(1)}, bf16[384,8,48]{0,2,1:T(8,128)(2,1)}, u32[]{:S(2)}) copy-start(bf16[384,8,48]{0,2,1:T(8,128)(2,1)} %slice.91) | copy-start | bytes 884740
  191.3 13.1 %copy-start.29 = (bf16[8,1,16,384]{3,2,1,0:T(8,128)(2,1)}, bf16[8,1,16,384]{3,2,1,0:T(8,128)(2,1)S(1)}, u32[]{:S(2)}) copy-start(bf16[8,1,16,384]{3,2,1,0:T(8,128)(2,1)S(1)} %all-to-all-done) | copy-start | bytes 294916
  191.3 11.1 %all-to-all-start.2 = ((bf16[32,1,4,384]{3,2,1,0:T(4,128)(2,1)}), bf16[32,1,4,384]{3,2,1,0:T(4,128)(2,1)S(1)}, u32[]{:S(2)}, u32[]{:S(2)}) async-start(bf16[32,1,4,384]{3,2,1,0:T(4,128)(2,1)} %copy.534), calls=%async_computation.2 | async-start | bytes 196608 | tf_op jit(solution)/shard_map/all_to_all | solution.py:68
  205.6 2.3 copy-start.44
  217.4 2.8 copy-start.32
  217.4 2.8 copy-start.36
  224.9 2.5 copy-start.56
  247.5 2.9 copy-start.22
  250.6 2.5 copy-start.3
  253.1 4.9 %copy-start.47 = (f32[4,32,6]{1,0,2:T(4,128)S(1)}, f32[4,32,6]{1,0,2:T(4,128)}, u32[]{:S(2)}) copy-start(f32[4,32,6]{1,0,2:T(4,128)} %copy.551) | copy-start | bytes 9220
  258.8 5.0 %copy-start.52 = (f32[4,32,6]{1,2,0:T(8,128)S(1)}, f32[4,32,6]{1,2,0:T(8,128)}, u32[]{:S(2)}) copy-start(f32[4,32,6]{1,2,0:T(8,128)} %copy.570) | copy-start | bytes 9220
  265.1 4.6 %copy-start.59 = (f32[4,32]{1,0:T(4,128)S(1)}, f32[4,32]{1,0:T(4,128)}, u32[]{:S(2)}) copy-start(f32[4,32]{1,0:T(4,128)} %copy-done.58) | copy-start | bytes 1540
  265.2 4.6 %copy-start.57 = (f32[4,32]{1,0:T(4,128)S(1)}, f32[4,32]{1,0:T(4,128)}, u32[]{:S(2)}) copy-start(f32[4,32]{1,0:T(4,128)} %copy-done.56) | copy-start | bytes 1540
  269.7 3.4 %copy-start.15 = (f32[32,6,4,4]{2,3,1,0:T(4,128)S(1)}, f32[32,6,4,4]{2,3,1,0:T(4,128)}, u32[]{:S(2)}) copy-start(f32[32,6,4,4]{2,3,1,0:T(4,128)} %copy-done.14) | copy-start | bytes 36868
  269.7 3.4 %copy-start.40 = (f32[32,6,4]{2,1,0:T(8,128)S(1)}, f32[32,6,4]{2,1,0:T(8,128)}, u32[]{:S(2)}) copy-start(f32[32,6,4]{2,1,0:T(8,128)} %multiply_divide_fusion) | copy-start | bytes 9220
  269.9 4.9 %copy-start.19 = (f32[32,6,4]{2,1,0:T(8,128)S(1)}, f32[32,6,4]{2,1,0:T(8,128)}, u32[]{:S(2)}) copy-start(f32[32,6,4]{2,1,0:T(8,128)} %copy-done.18) | copy-start | bytes 9220
  273.1 2.4 copy-start.35
  279.9 3.9 %copy-start.54 = (f32[4,6,32]{2,1,0:T(8,128)S(1)}, f32[4,6,32]{2,1,0:T(8,128)}, u32[]{:S(2)}) copy-start(f32[4,6,32]{2,1,0:T(8,128)} %copy-done.53) | copy-start | bytes 9220
  279.9 11.5 %copy-start.10 = (bf16[384,8,48]{0,2,1:T(8,128)(2,1)S(1)}, bf16[384,8,48]{0,2,1:T(8,128)(2,1)}, u32[]{:S(2)}) copy-start(bf16[384,8,48]{0,2,1:T(8,128)(2,1)} %slice.91) | copy-start | bytes 884740
  280.0 11.9 %copy-start.17 = (f32[4,6,32,32]{2,3,1,0:T(8,128)S(1)}, f32[4,6,32,32]{2,3,1,0:T(8,128)}, u32[]{:S(2)}) copy-start(f32[4,6,32,32]{2,3,1,0:T(8,128)} %copy-done.16) | copy-start | bytes 294916
  280.5 11.5 %copy-start.21 = (bf16[32,4,6,64]{3,2,0,1:T(8,128)(2,1)S(1)}, bf16[32,4,6,64]{3,2,0,1:T(8,128)(2,1)}, u32[]{:S(2)}) copy-start(bf16[32,4,6,64]{3,2,0,1:T(8,128)(2,1)} %convert_element_type.403) | copy-start | bytes 294916
  281.2 10.2 %all-to-all-start.3 = ((bf16[32,1,4,384]{3,2,1,0:T(4,128)(2,1)}), bf16[32,1,4,384]{3,2,1,0:T(4,128)(2,1)S(1)}, u32[]{:S(2)}, u32[]{:S(2)}) async-start(bf16[32,1,4,384]{3,2,1,0:T(4,128)(2,1)} %bitcast.70), calls=%async_computation.3 | async-start | bytes 196608 | tf_op jit(solution)/shard_map/all_to_all | solution.py:79
  (35 other events, 42.7 us)
Sparse Core Ops, SparseCore 0:
  10.2 57.8 all-gather.8
  71.0 53.9 all-gather.10
  127.9 53.9 all-gather.6
where the time goes:
time: 312 us; the launch traced here: 310 us
  waiting for transfers between devices  146 us (47%)
  local copies, waits for them, and re-layouts  76.9 us (25%)
  other arithmetic  27.8 us (9%)
  matrix products  17.5 us (6%)
  blocking collectives  15 us (5%)
  between operations  14.4 us (5%)
  starting transfers between devices  12.2 us (4%)
    all_gather x3, waiting for transfers between devices, full_weights(): got = lax.all_gather(cat, ALL, axis=0, tiled=False)  133 us
    reshape x3, local copies, waits for them, and re-layouts, full_weights(): got = got.reshape(nz, ny, nx, din, cat.shape[1])  8.39 us
    all_to_all x1, blocking collectives, local(): depth_act = lax.all_to_all(volume, 'gz', 2, 0, tiled=True)  8.33 us
    reshape x9, local copies, waits for them, and re-layouts, sublayer(): key_part = head_norm(packed[..., feat_len:2 * feat_len].reshape(head_shape))  8.21 us
    rsqrt x12, local copies, waits for them, and re-layouts, head_norm(): lax.rsqrt(jnp.mean(vector * vector, axis=-1, keepdims=True) + 1e-06)  8.07 us
    all_to_all x1, waiting for transfers between devices, from_planes(): return lax.all_to_all(parts, ALL, 0, 0, tiled=True)  7.56 us
    reshape x9, local copies, waits for them, and re-layouts, sublayer(): queries = head_norm(packed[..., :feat_len].reshape(head_shape))  7.11 us
    all_to_all x1, blocking collectives, local(): return lax.all_to_all(grad_zero, 'gz', 0, 2, tiled=True)  6.67 us
  transfers between devices with their start and end apart: 6, of which 5 were waited for; matrix products, arithmetic and copies ran while one was open for 12% of the time, Pallas kernels for 0%

commit v1 on v0

--- a/solution.py
+++ b/solution.py
@@ -99,7 +99,10 @@
     grad_plane = plane_pullback(cot_plane)[0]
     grad_one = from_planes(grad_plane, sizes)
     grad_zero = depth_pullback(grad_one)[0]
-    return lax.all_to_all(grad_zero, "gz", 0, 2, tiled=True)
+    return jnp.concatenate(
+        lax.all_to_all(jnp.stack(jnp.split(grad_zero, lax.axis_size("gz"), axis=0)), "gz", 0, 0),
+        axis=2,
+    )
 
 
 def along_rows(member, w_inner, w_outer):

time: 312 us -> 312 us (level)
  no operation moved by 1% of the time
where the time goes in v1:
time: 312 us; the launch traced here: 310 us
  waiting for transfers between devices  147 us (47%)
  local copies, waits for them, and re-layouts  76.6 us (25%)
  other arithmetic  27.8 us (9%)
  matrix products  17.5 us (6%)
  blocking collectives  15 us (5%)
  between operations  14.4 us (5%)
  starting transfers between devices  12.2 us (4%)
    all_gather x3, waiting for transfers between devices, full_weights(): got = lax.all_gather(cat, ALL, axis=0, tiled=False)  133 us
    reshape x3, local copies, waits for them, and re-layouts, full_weights(): got = got.reshape(nz, ny, nx, din, cat.shape[1])  8.39 us
    all_to_all x1, blocking collectives, local(): depth_act = lax.all_to_all(volume, 'gz', 2, 0, tiled=True)  8.33 us
    reshape x9, local copies, waits for them, and re-layouts, sublayer(): key_part = head_norm(packed[..., feat_len:2 * feat_len].reshape(head_shape))  8.21 us
    rsqrt x12, local copies, waits for them, and re-layouts, head_norm(): lax.rsqrt(jnp.mean(vector * vector, axis=-1, keepdims=True) + 1e-06)  8.03 us
    all_to_all x1, waiting for transfers between devices, from_planes(): return lax.all_to_all(parts, ALL, 0, 0, tiled=True)  7.56 us
    reshape x9, local copies, waits for them, and re-layouts, sublayer(): queries = head_norm(packed[..., :feat_len].reshape(head_shape))  7.11 us
    all_to_all x1, blocking collectives, local(): lax.all_to_all(jnp.stack(jnp.split(grad_zero, lax.axis_size('gz'), axis=0...  6.67 us
  transfers between devices with their start and end apart: 6, of which 5 were waited for; matrix products, arithmetic and copies ran while one was open for 12% of the time, Pallas kernels for 0%

profile of v1, /device:TPU:0, one launch (start us, length us, event | category | flops | bytes accessed | tf_op | source)
XLA Modules:
  0.0 310.0 jit_solution(10911965370553076256)
XLA Ops:
  11.9 8.3 %all_to_all.29 = bf16[8,1,16,384]{3,0,1,2:T(8,128)(2,1)S(1)} all-to-all(bf16[8,1,16,384]{3,0,1,2:T(8,128)(2,1)S(1)} %copy.512), channel_id=1, replica_groups=mesh['gz'=4,'gy'=4,'gx'=2] {'gz'}, dimensions={2} | all-to-all | bytes 196608 | tf_op jit(solution)/shard_map/all_to_all | solution.py:94
  20.3 5.8 %all-to-all-start = ((bf16[8,1,16,384]{3,2,1,0:T(8,128)(2,1)}), bf16[8,1,16,384]{3,2,1,0:T(8,128)(2,1)S(1)}, u32[]{:S(2)}, u32[]{:S(2)}) async-start(bf16[8,1,16,384]{3,2,1,0:T(8,128)(2,1)} %param.5), calls=%async_computation | async-start | bytes 196608 | tf_op jit(solution)/shard_map/all_to_all | solution.py:85
  26.9 41.2 %all-gather.9.cloned.1.call-done = bf16[3072,192]{1,0:T(8,128)(2,1)} async-done(((bf16[96,192]{1,0:T(8,128)(2,1)}), bf16[3072,192]{1,0:T(8,128)(2,1)}) %all-gather.9.cloned.1.call-update) | async-done | bytes 1179664 | tf_op jit(solution)/shard_map/all_gather | solution.py:46
  68.1 2.8 copy.518
  75.3 1.8 convert_element_type.405
  85.7 39.3 %all-gather.11.cloned.1.call-done = bf16[3072,192]{1,0:T(8,128)(2,1)} async-done(((bf16[96,192]{1,0:T(8,128)(2,1)}), bf16[3072,192]{1,0:T(8,128)(2,1)}) %all-gather.11.cloned.1.call-update) | async-done | bytes 1179664 | tf_op jit(solution)/shard_map/all_gather | solution.py:46
  125.0 2.8 copy.534
  129.7 52.1 %all-gather.7.cloned.1.call-done = bf16[3072,192]{1,0:T(8,128)(2,1)} async-done(((bf16[96,192]{1,0:T(8,128)(2,1)}), bf16[3072,192]{1,0:T(8,128)(2,1)}) %all-gather.7.cloned.1.call-update) | async-done | bytes 1179664 | tf_op jit(solution)/shard_map/all_gather | solution.py:46
  181.9 2.8 copy.510
  184.7 1.9 reshape.959
  191.3 3.7 %all-to-all-start.2 = ((bf16[32,1,4,384]{3,2,1,0:T(4,128)(2,1)}), bf16[32,1,4,384]{3,2,1,0:T(4,128)(2,1)S(1)}, u32[]{:S(2)}, u32[]{:S(2)}) async-start(bf16[32,1,4,384]{3,2,1,0:T(4,128)(2,1)} %copy.530), calls=%async_computation.2 | async-start | bytes 196608 | tf_op jit(solution)/shard_map/all_to_all | solution.py:68
  196.1 6.3 %all-to-all-done.2 = bf16[32,1,4,384]{3,2,1,0:T(4,128)(2,1)S(1)} async-done(((bf16[32,1,4,384]{3,2,1,0:T(4,128)(2,1)}), bf16[32,1,4,384]{3,2,1,0:T(4,128)(2,1)S(1)}, u32[]{:S(2)}, u32[]{:S(2)}) %all-to-all-start.2) | async-done | bytes 98336 | tf_op jit(solution)/shard_map/all_to_all | solution.py:68
  214.3 1.8 convert_element_type.420
  221.7 1.8 reshape.980
  227.3 1.9 reshape.984
  229.2 1.9 multiply_reduce_fusion.1
  234.6 1.8 reshape.983
  236.5 1.9 reshape.986
  238.4 1.9 multiply_reduce_fusion
  243.8 1.8 reshape.985
  245.6 1.8 convert_element_type.436
  251.3 1.7 multiply_reduce_fusion.10
  253.0 1.6 multiply_reduce_fusion.11
  255.3 1.8 reshape.987
  261.7 1.9 reshape.988
  266.1 1.9 reshape.989
  267.9 1.6 multiply_reduce_fusion.14
  270.9 2.0 fusion.14
  273.0 1.6 multiply_reduce_fusion.9
  281.0 2.6 all-to-all-start.3
  283.7 7.6 %all-to-all-done.3 = bf16[32,1,4,384]{3,2,1,0:T(4,128)(2,1)S(1)} async-done(((bf16[32,1,4,384]{3,2,1,0:T(4,128)(2,1)}), bf16[32,1,4,384]{3,2,1,0:T(4,128)(2,1)S(1)}, u32[]{:S(2)}, u32[]{:S(2)}) %all-to-all-start.3) | async-done | bytes 98336 | tf_op jit(solution)/shard_map/all_to_all | solution.py:79
  296.2 6.7 %all_to_all.30 = bf16[4,8,1,4,384]{4,1,3,2,0:T(8,128)(2,1)S(1)} all-to-all(bf16[4,8,1,4,384]{4,1,3,2,0:T(8,128)(2,1)S(1)} %pad_maximum_fusion), channel_id=1, replica_groups=mesh['gz'=4,'gy'=4,'gx'=2] {'gz'}, dimensions={0} | all-to-all | bytes 196608 | tf_op jit(solution)/shard_map/all_to_all | solution.py:103
  (292 shorter events, 79.4 us)
Async XLA Ops:
  6.5 61.5 %all-gather.9.cloned.1.call-start = ((), (), s32[]{:S(2)}) async-start(), calls=%async_computation.6 | async-start | bytes 1622016 | tf_op jit(solution)/shard_map/all_gather | solution.py:46
  9.0 115.9 %all-gather.11.cloned.1.call-start = ((), (), s32[]{:S(2)}) async-start(), calls=%async_computation.7 | async-start | bytes 1622016 | tf_op jit(solution)/shard_map/all_gather | solution.py:46
  10.0 171.8 %all-gather.7.cloned.1.call-start = ((), (), s32[]{:S(2)}) async-start(), calls=%async_computation.5 | async-start | bytes 1622016 | tf_op jit(solution)/shard_map/all_gather | solution.py:46
  20.3 170.1 %copy-start.11 = (bf16[8,1,16,384]{3,0,1,2:T(8,128)(2,1)}, bf16[8,1,16,384]{3,0,1,2:T(8,128)(2,1)S(1)}, u32[]{:S(2)}) copy-start(bf16[8,1,16,384]{3,0,1,2:T(8,128)(2,1)S(1)} %all_to_all.29) | copy-start | bytes 294916
  20.3 171.1 %all-to-all-start = ((bf16[8,1,16,384]{3,2,1,0:T(8,128)(2,1)}), bf16[8,1,16,384]{3,2,1,0:T(8,128)(2,1)S(1)}, u32[]{:S(2)}, u32[]{:S(2)}) async-start(bf16[8,1,16,384]{3,2,1,0:T(8,128)(2,1)} %param.5), calls=%async_computation | async-start | bytes 196608 | tf_op jit(solution)/shard_map/all_to_all | solution.py:85
  74.0 9.7 %copy-start = (f32[1,32,4,6,64]{4,3,1,2,0:T(8,128)}, f32[1,32,4,6,64]{4,3,1,2,0:T(8,128)S(1)}, u32[]{:S(2)}) copy-start(f32[1,32,4,6,64]{4,3,1,2,0:T(8,128)S(1)} %reshape.969) | copy-start | bytes 589828
  84.0 41.0 %copy-start.16 = (f32[4,6,32,32]{2,3,1,0:T(8,128)}, f32[4,6,32,32]{2,3,1,0:T(8,128)S(1)}, u32[]{:S(2)}) copy-start(f32[4,6,32,32]{2,3,1,0:T(8,128)S(1)} %get-tuple-element.30) | copy-start | bytes 294916
  84.0 43.8 %copy-start.53 = (f32[4,6,32]{2,1,0:T(8,128)}, f32[4,6,32]{2,1,0:T(8,128)S(1)}, u32[]{:S(2)}) copy-start(f32[4,6,32]{2,1,0:T(8,128)S(1)} %get-tuple-element.29) | copy-start | bytes 9220
  186.5 2.9 copy-start.41
  186.6 3.5 %copy-start.38 = (bf16[1,32,4,6,64]{4,1,3,2,0:T(8,128)(2,1)S(1)}, bf16[1,32,4,6,64]{4,1,3,2,0:T(8,128)(2,1)}, u32[]{:S(2)}) copy-start(bf16[1,32,4,6,64]{4,1,3,2,0:T(8,128)(2,1)} %fusion.6) | copy-start | bytes 294916
  186.6 3.8 %copy-start.9 = (bf16[384,8,48]{0,2,1:T(8,128)(2,1)S(1)}, bf16[384,8,48]{0,2,1:T(8,128)(2,1)}, u32[]{:S(2)}) copy-start(bf16[384,8,48]{0,2,1:T(8,128)(2,1)} %slice.95) | copy-start | bytes 884740
  191.3 13.1 %copy-start.29 = (bf16[8,1,16,384]{3,2,1,0:T(8,128)(2,1)}, bf16[8,1,16,384]{3,2,1,0:T(8,128)(2,1)S(1)}, u32[]{:S(2)}) copy-start(bf16[8,1,16,384]{3,2,1,0:T(8,128)(2,1)S(1)} %all-to-all-done) | copy-start | bytes 294916
  191.3 11.1 %all-to-all-start.2 = ((bf16[32,1,4,384]{3,2,1,0:T(4,128)(2,1)}), bf16[32,1,4,384]{3,2,1,0:T(4,128)(2,1)S(1)}, u32[]{:S(2)}, u32[]{:S(2)}) async-start(bf16[32,1,4,384]{3,2,1,0:T(4,128)(2,1)} %copy.530), calls=%async_computation.2 | async-start | bytes 196608 | tf_op jit(solution)/shard_map/all_to_all | solution.py:68
  205.6 2.3 copy-start.44
  217.4 2.8 copy-start.32
  217.4 2.9 copy-start.36
  224.8 2.5 copy-start.56
  247.4 2.9 copy-start.22
  250.5 2.5 copy-start.3
  253.0 4.9 %copy-start.47 = (f32[4,32,6]{1,0,2:T(4,128)S(1)}, f32[4,32,6]{1,0,2:T(4,128)}, u32[]{:S(2)}) copy-start(f32[4,32,6]{1,0,2:T(4,128)} %copy.547) | copy-start | bytes 9220
  258.6 5.0 %copy-start.52 = (f32[4,32,6]{1,2,0:T(8,128)S(1)}, f32[4,32,6]{1,2,0:T(8,128)}, u32[]{:S(2)}) copy-start(f32[4,32,6]{1,2,0:T(8,128)} %copy.566) | copy-start | bytes 9220
  265.0 4.6 %copy-start.59 = (f32[4,32]{1,0:T(4,128)S(1)}, f32[4,32]{1,0:T(4,128)}, u32[]{:S(2)}) copy-start(f32[4,32]{1,0:T(4,128)} %copy-done.58) | copy-start | bytes 1540
  265.0 4.6 %copy-start.57 = (f32[4,32]{1,0:T(4,128)S(1)}, f32[4,32]{1,0:T(4,128)}, u32[]{:S(2)}) copy-start(f32[4,32]{1,0:T(4,128)} %copy-done.56) | copy-start | bytes 1540
  269.6 3.4 %copy-start.15 = (f32[32,6,4,4]{2,3,1,0:T(4,128)S(1)}, f32[32,6,4,4]{2,3,1,0:T(4,128)}, u32[]{:S(2)}) copy-start(f32[32,6,4,4]{2,3,1,0:T(4,128)} %copy-done.14) | copy-start | bytes 36868
  269.6 3.4 %copy-start.40 = (f32[32,6,4]{2,1,0:T(8,128)S(1)}, f32[32,6,4]{2,1,0:T(8,128)}, u32[]{:S(2)}) copy-start(f32[32,6,4]{2,1,0:T(8,128)} %multiply_divide_fusion) | copy-start | bytes 9220
  269.8 4.8 %copy-start.19 = (f32[32,6,4]{2,1,0:T(8,128)S(1)}, f32[32,6,4]{2,1,0:T(8,128)}, u32[]{:S(2)}) copy-start(f32[32,6,4]{2,1,0:T(8,128)} %copy-done.18) | copy-start | bytes 9220
  272.9 2.4 copy-start.35
  279.8 3.9 %copy-start.54 = (f32[4,6,32]{2,1,0:T(8,128)S(1)}, f32[4,6,32]{2,1,0:T(8,128)}, u32[]{:S(2)}) copy-start(f32[4,6,32]{2,1,0:T(8,128)} %copy-done.53) | copy-start | bytes 9220
  279.8 11.5 %copy-start.10 = (bf16[384,8,48]{0,2,1:T(8,128)(2,1)S(1)}, bf16[384,8,48]{0,2,1:T(8,128)(2,1)}, u32[]{:S(2)}) copy-start(bf16[384,8,48]{0,2,1:T(8,128)(2,1)} %slice.95) | copy-start | bytes 884740
  279.8 11.9 %copy-start.17 = (f32[4,6,32,32]{2,3,1,0:T(8,128)S(1)}, f32[4,6,32,32]{2,3,1,0:T(8,128)}, u32[]{:S(2)}) copy-start(f32[4,6,32,32]{2,3,1,0:T(8,128)} %copy-done.16) | copy-start | bytes 294916
  280.3 11.5 %copy-start.21 = (bf16[32,4,6,64]{3,2,0,1:T(8,128)(2,1)S(1)}, bf16[32,4,6,64]{3,2,0,1:T(8,128)(2,1)}, u32[]{:S(2)}) copy-start(bf16[32,4,6,64]{3,2,0,1:T(8,128)(2,1)} %convert_element_type.405) | copy-start | bytes 294916
  281.0 10.2 %all-to-all-start.3 = ((bf16[32,1,4,384]{3,2,1,0:T(4,128)(2,1)}), bf16[32,1,4,384]{3,2,1,0:T(4,128)(2,1)S(1)}, u32[]{:S(2)}, u32[]{:S(2)}) async-start(bf16[32,1,4,384]{3,2,1,0:T(4,128)(2,1)} %bitcast.70), calls=%async_computation.3 | async-start | bytes 196608 | tf_op jit(solution)/shard_map/all_to_all | solution.py:79
  (35 other events, 42.6 us)
Sparse Core Ops, SparseCore 0:
  10.2 57.8 all-gather.8
  71.0 53.9 all-gather.10
  127.9 53.9 all-gather.6
